TPU v7x, 128 devices: a whole 4x4x4 slice. The times are simulated.
128 devices in a mesh: req: 8 (over x, core), kv: 16 (over y, z).
Axes of the slice: x: 4, y: 4, z: 4, core: 2. Of those that a mesh axis runs over, the one named last changes fastest.
Arguments:
- x_steps: bfloat16 [4, 1024, 1536], P(None, ('req', 'kv')), may hold values from -6 to 6
- lengths: int32 [128], replicated, may hold values from 16 to 8192
- perm: int32 [128], replicated, may hold values from 0 to 127, as said below
- parents: int32 [4, 1024], replicated, may hold values from 0 to 7
- table: int32 [1024, 9], P(('req', 'kv')), may hold values from 0 to 9215, as said below
- pool: bfloat16 [9216, 128, 256], P(('req', 'kv')), may hold values from -900 to 900
- norm_attn: float32 [1536], replicated, may hold values from 0.1 to 1.9
- w_query: bfloat16 [1536, 1536], replicated, may hold values from -0.15625 to 0.15625
- w_keyval: bfloat16 [1536, 256], replicated, may hold values from -0.15625 to 0.15625
- w_out: bfloat16 [1536, 1536], replicated, may hold values from -0.15625 to 0.15625
- norm_mlp: float32 [1536], replicated, may hold values from 0.1 to 1.9
- w_gate: bfloat16 [1536, 4608], P(None, 'kv'), may hold values from -0.15625 to 0.15625
- w_up: bfloat16 [1536, 4608], P(None, 'kv'), may hold values from -0.15625 to 0.15625
- w_down: bfloat16 [4608, 1536], P('kv'), may hold values from -0.09375 to 0.09375
Outputs:
- outputs: bfloat16 [4, 1024, 1536], P(None, ('req', 'kv'))
Inputs may be any that keep to these rules, and one draw needn't show every extreme that they name: perm is a permutation with perm[s] % 16 == s % 16; among the 8 slots s with one s // 16 and one s % 16 // 8, every req index occurs as perm[s] // 16 exactly once. The entries of row b lie in [(b // 8) * 72, (b // 8 + 1) * 72); no page appears twice in the table.
All inputs are finite; a program needn't handle non-finite values.
Results may differ from a plain program's by a relative error of at most 0.02.
Values may be sent and summed in bfloat16 or wider, within the bound.
No kernel may reach another device: no remote copies, remote signals or barrier semaphores. Data moves between devices by JAX's collectives and lax.ppermute only.
A program may use at most 192 MiB of HBM per device.

v0:
```python
import jax
import jax.numpy as jnp
from jax import lax
from jax.sharding import PartitionSpec as P

WINDOW = 1024
PAGE = 128
BEAMS = 8
EPSILON = 1e-06
NEGATIVE = -1e30


def member_of(beam_index, half_index, halves):
    return beam_index % 2 + 2 * half_index + 2 * halves * (beam_index // 2)


def rms_round(values, gain):
    wide = values.astype(jnp.float32)
    mean_square = jnp.mean(wide * wide, axis=-1, keepdims=True)
    return (wide * lax.rsqrt(mean_square + EPSILON) * gain).astype(jnp.bfloat16)


def rank_within(labels, offsets):
    earlier = (labels[None, :] == labels[:, None]) & (offsets[None, :] < offsets[:, None])
    return jnp.sum(earlier.astype(jnp.int32), axis=1)


def follow(index, table):
    picks = index[:, None, :] == jnp.arange(BEAMS, dtype=jnp.int32)[None, :, None]
    return jnp.sum(jnp.where(picks, table[None, :, :], 0), axis=1)


def pick_rows(index, table):
    picks = index[:, None, :] == jnp.arange(BEAMS, dtype=jnp.int32)[None, :, None]
    return jnp.sum(jnp.where(picks[..., None], table[None, :, :, :], 0), axis=1).astype(table.dtype)


def on_device(
    x_steps,
    lengths,
    perm,
    parents,
    table,
    pool,
    norm_attn,
    w_query,
    w_keyval,
    w_out,
    norm_mlp,
    w_gate,
    w_up,
    w_down,
):
    steps, rows, width = x_steps.shape
    head_dim = pool.shape[2] // 2
    heads = w_query.shape[1] // head_dim
    qwidth = heads * head_dim
    span = table.shape[1] * pool.shape[1]
    req_count = lax.axis_size("req")
    kv_count = lax.axis_size("kv")
    group = lax.axis_index("req")
    member = lax.axis_index("kv")
    halves = kv_count // BEAMS
    half = member // 2 % halves
    beam = member % 2 + 2 * (member // (2 * halves))
    per_group = halves * rows
    group_rows = kv_count * rows
    quota = rows // req_count
    offsets = jnp.arange(rows, dtype=jnp.int32)
    slot_ids = group * per_group + half * rows + offsets
    placed = lax.dynamic_slice_in_dim(perm.reshape(req_count, per_group), half * rows, rows, 1)
    serving = lax.dynamic_index_in_dim(placed, group, 0, keepdims=False)
    target = jnp.sum(
        jnp.where(placed == slot_ids[None, :], jnp.arange(req_count, dtype=jnp.int32)[:, None], 0),
        axis=0,
    )
    anchor = serving // per_group
    send_order = jnp.argsort(target * rows + offsets)
    outgoing = x_steps[:, send_order].reshape(steps, req_count, quota, width)
    arrived = lax.all_to_all(outgoing, "req", split_axis=1, concat_axis=1, tiled=True).reshape(
        steps, rows, width
    )
    inputs = arrived[:, anchor * quota + rank_within(anchor, offsets)]
    normed = rms_round(inputs.reshape(steps * rows, width), norm_attn)
    query = jnp.dot(normed, w_query, preferred_element_type=jnp.float32).astype(jnp.bfloat16)
    fresh = jnp.dot(normed, w_keyval, preferred_element_type=jnp.float32).astype(jnp.bfloat16)
    packed = jnp.concatenate([query, fresh], axis=-1).reshape(steps, rows, qwidth + 2 * head_dim)
    gathered = lax.all_gather(packed, "kv", axis=0)
    mine = gathered.reshape((BEAMS // 2, halves, 2) + packed.shape)
    mine = lax.dynamic_index_in_dim(mine, half, 1, keepdims=False).reshape((BEAMS,) + packed.shape)
    queries = mine[..., :qwidth].reshape(BEAMS, steps, rows, heads, head_dim)
    entries = mine[..., qwidth:]
    family = lax.dynamic_slice_in_dim(parents, group * group_rows, group_rows, 1).reshape(
        (steps, BEAMS // 2, halves, 2, rows)
    )
    family = lax.dynamic_index_in_dim(family, half, 2, keepdims=False).reshape(steps, BEAMS, rows)
    own = jnp.broadcast_to(jnp.arange(BEAMS, dtype=jnp.int32)[:, None], (BEAMS, rows))
    cache_beam = own
    sources = []
    cache_beams = []
    listed = []
    for step_index in range(steps):
        cache_beam = follow(family[step_index], cache_beam)
        sources = [follow(family[step_index], source) for source in sources] + [own]
        cache_beams.append(cache_beam)
        picked = [pick_rows(source, entries[:, s]) for s, source in enumerate(sources)]
        picked += [jnp.zeros_like(picked[0])] * (steps - 1 - step_index)
        listed.append(jnp.stack(picked))
    held = jnp.stack(cache_beams, axis=1) == beam
    listed = jnp.stack(listed)
    length = lengths[serving]
    first_page = jnp.maximum(length - WINDOW + 1, 0) // PAGE
    key_pos = first_page[:, None] * PAGE + jnp.arange(span, dtype=jnp.int32)[None, :]
    device = group * kv_count + member
    pages = pool[table - device * pool.shape[0]].reshape(rows, span, 2 * head_dim)
    keys = pages[:, :, :head_dim]
    values = pages[:, :, head_dim:]
    scale = head_dim ** (-0.5)
    scores = (
        jnp.einsum("jtrhd,rkd->jtrhk", queries, keys, preferred_element_type=jnp.float32) * scale
    )
    step_ids = jnp.arange(steps, dtype=jnp.int32)
    allowed = (key_pos[None, :, :] < length[None, :, None]) & (
        key_pos[None, :, :] > length[None, :, None] + step_ids[:, None, None] - WINDOW
    )
    scores = jnp.where(allowed[None, :, :, None, :], scores, NEGATIVE)
    high_c = jnp.max(scores, axis=-1)
    weights = jnp.exp(scores - high_c[..., None]).astype(jnp.bfloat16)
    total_c = jnp.sum(weights.astype(jnp.float32), axis=-1)
    sum_c = jnp.einsum("jtrhk,rkd->jtrhd", weights, values, preferred_element_type=jnp.float32)
    new_keys = listed[..., :head_dim]
    new_values = listed[..., head_dim:]
    fresh_scores = (
        jnp.einsum("jtrhd,tsjrd->jtrhs", queries, new_keys, preferred_element_type=jnp.float32)
        * scale
    )
    counted = step_ids[None, :] <= step_ids[:, None]
    fresh_scores = jnp.where(counted[None, :, None, None, :], fresh_scores, NEGATIVE)
    high_n = jnp.max(fresh_scores, axis=-1)
    fresh_weights = jnp.exp(fresh_scores - high_n[..., None]).astype(jnp.bfloat16)
    fresh_weights = jnp.where(counted[None, :, None, None, :], fresh_weights, 0)
    total_n = jnp.sum(fresh_weights.astype(jnp.float32), axis=-1)
    sum_n = jnp.einsum(
        "jtrhs,tsjrd->jtrhd", fresh_weights, new_values, preferred_element_type=jnp.float32
    )
    highest = jnp.maximum(high_c, high_n)
    scale_c = jnp.exp(high_c - highest)
    scale_n = jnp.exp(high_n - highest)
    totals = total_c * scale_c + total_n * scale_n
    weighted = sum_c * scale_c[..., None] + sum_n * scale_n[..., None]
    attended = (
        (weighted / totals[..., None]).astype(jnp.bfloat16).reshape(BEAMS, steps, rows, qwidth)
    )
    attended = jnp.where(held[..., None], attended, jnp.zeros_like(attended))
    spread = attended.reshape(BEAMS // 2, 1, 2, steps, rows, qwidth)
    in_half = (jnp.arange(halves, dtype=jnp.int32) == half)[None, :, None, None, None, None]
    outgoing_att = jnp.where(in_half, spread, jnp.zeros_like(spread)).reshape(
        kv_count, steps, rows, qwidth
    )
    received = lax.all_to_all(outgoing_att, "kv", split_axis=0, concat_axis=0, tiled=True)
    attended_own = jnp.sum(received.astype(jnp.float32), axis=0).astype(jnp.bfloat16)
    current = inputs.reshape(steps * rows, width)
    residual = (
        current.astype(jnp.float32)
        + jnp.dot(
            attended_own.reshape(steps * rows, qwidth), w_out, preferred_element_type=jnp.float32
        )
    ).astype(jnp.bfloat16)
    mlp_in = lax.all_gather(rms_round(residual, norm_mlp), "kv", axis=0, tiled=True)
    gate = jnp.dot(mlp_in, w_gate, preferred_element_type=jnp.float32)
    upward = jnp.dot(mlp_in, w_up, preferred_element_type=jnp.float32)
    hidden = (jax.nn.gelu(gate, approximate=True) * upward).astype(jnp.bfloat16)
    terms = jnp.dot(hidden, w_down, preferred_element_type=jnp.float32).astype(jnp.bfloat16)
    terms = terms.reshape(kv_count, steps * rows, width)
    partial = lax.all_to_all(terms, "kv", split_axis=0, concat_axis=0, tiled=True)
    summed = jnp.sum(partial.astype(jnp.float32), axis=0)
    finished = (
        (residual.astype(jnp.float32) + summed).astype(jnp.bfloat16).reshape(steps, rows, width)
    )
    back_order = jnp.argsort(anchor * rows + offsets)
    leaving = finished[:, back_order].reshape(steps, req_count, quota, width)
    returned = lax.all_to_all(leaving, "req", split_axis=1, concat_axis=1, tiled=True).reshape(
        steps, rows, width
    )
    return returned[:, target * quota + rank_within(target, offsets)]


def solution(mesh):
    in_specs = (
        P(None, ("req", "kv"), None),
        P(),
        P(),
        P(),
        P(("req", "kv"), None),
        P(("req", "kv"), None, None),
        P(),
        P(),
        P(),
        P(),
        P(),
        P(None, "kv"),
        P(None, "kv"),
        P("kv", None),
    )
    out_specs = P(None, ("req", "kv"), None)
    return jax.shard_map(
        on_device, mesh=mesh, in_specs=in_specs, out_specs=out_specs, check_vma=False
    )
```

profile of v0, /device:TPU:1, one launch (start us, length us, event | category | flops | bytes accessed | tf_op | source)
XLA Modules:
  0.0 238.4 jit_solution(9731133063465071926)
XLA Ops:
  6.5 0.8 reshape.452
  7.5 1.0 sort.31
  8.5 1.7 gather_fusion
  10.3 0.7 copy.127
  10.9 5.8 %all-to-all-start = ((bf16[4,8,1,1536]{3,0,2,1:T(4,128)(2,1)}), bf16[4,8,1,1536]{3,0,2,1:T(4,128)(2,1)S(1)}, u32[]{:S(2)}, u32[]{:S(2)}) async-start(bf16[4,8,1,1536]{3,0,2,1:T(4,128)(2,1)} %copy.127), calls=%async_computation | async-start | bytes 196608 | tf_op jit(solution)/shard_map/all_to_all | solution.py:80
  16.9 0.7 compare_select_fusion
  17.7 0.2 convert_reduce_fusion.4
  17.9 0.7 constant_dynamic-slice_fusion.4
  18.8 1.3 gather_fusion.3
  20.2 1.6 all-to-all-done
  21.7 0.6 gather_fusion.1
  22.4 0.1 multiply_reduce_fusion.1
  22.7 1.4 convolution_convert_fusion.2
  24.1 3.3 %convolution_convert_fusion.1 = bf16[32,1536]{1,0:T(8,128)(2,1)S(1)} fusion(bf16[1536,1536]{1,0:T(8,128)(2,1)} %param.21, f32[4,8,1536]{2,0,1:T(4,128)S(1)} %convert_bitcast_fusion, f32[1536]{0:T(1024)} %param.20, f32[32]{0:T(128)S(1)} %rsqrt.20), kind=kOutput, calls=%fused_computation.19 | convolution fusion | flops 151191552 | bytes 5019776 | tf_op jit(solution)/shard_map/dot_general | solution.py:85
  27.5 0.7 maximum_bitcast_fusion.4
  28.2 7.8 %gather_fusion.2 = bf16[72,128,256]{2,1,0:T(8,128)(2,1)} fusion(bf16[72,128,256]{2,1,0:T(8,128)(2,1)} %param.19, s32[1024]{0:T(1024)S(1)} %pad_clamp_fusion.3), kind=kCustom, calls=%fused_computation.2 | custom fusion | bytes 9437472 | tf_op jit(solution)/shard_map/gather | solution.py:115
  36.7 35.6 %all-gather.3.cloned.1.call-done = bf16[16,4,8,1792]{3,2,1,0:T(8,128)(2,1)} async-done(((bf16[1,4,8,1792]{3,2,1,0:T(8,128)(2,1)}), bf16[16,4,8,1792]{3,2,1,0:T(8,128)(2,1)}) %all-gather.3.cloned.1.call-update) | async-done | bytes 1835024 | tf_op jit(solution)/shard_map/all_gather | solution.py:88
  72.3 1.4 constant_dynamic-slice_fusion.1
  73.8 0.8 select_reduce_fusion.9
  75.2 0.3 maximum_bitcast_fusion.3
  75.6 0.6 maximum_bitcast_fusion
  76.2 0.4 pad_maximum_fusion
  76.6 0.7 fusion.52
  77.3 0.6 convert_reduce_fusion.2
  77.9 1.9 fusion.25
  79.8 8.5 %fusion = (f32[8,4,8,12]{3,1,0,2:T(4,128)S(1)}, f32[8,1152,8,4,12]{1,4,3,2,0:T(8,128)}) fusion(pred[4,8,1152]{2,0,1:T(4,128)(4,1)S(1)} %compare_and_fusion, bf16[8,4,8,12,128]{4,2,3,1,0:T(8,128)(2,1)S(1)} %slice_bitcast_fusion.6, bf16[8,1152,256]{2,1,0:T(8,128)(2,1)S(1)} %bitcast.164), kind=kOutput, calls=%fused_computation.10 | convolution fusion | flops 916583424 | bytes 17350656 | tf_op jit(solution)/shard_map/jtrhd,rkd->jtrhk/dot_general | solution.py:120
  88.3 11.0 %convert_reduce_fusion = f32[8,4,8,12]{3,1,0,2:T(4,128)S(1)} fusion(f32[8,4,8,12]{3,1,0,2:T(4,128)S(1)} %get-tuple-element.56, f32[8,1152,8,4,12]{1,4,3,2,0:T(8,128)} %get-tuple-element.57, pred[4,8,1152]{2,0,1:T(4,128)(4,1)S(1)} %compare_and_fusion), kind=kLoop, calls=%fused_computation.8 | loop fusion | flops 17691648 | bytes 14217216 | tf_op jit(solution)/shard_map/reduce_sum | solution.py:129
  99.3 0.2 fusion.32
  99.6 9.7 %fusion.6 = bf16[8,4,8,12,128]{4,3,1,0,2:T(8,128)(2,1)S(1)} fusion(f32[8,4,8,12,128]{4,3,1,0,2:T(8,128)} %fusion.25, bf16[8,1152,256]{2,1,0:T(8,128)(2,1)} %bitcast.161, f32[8,1152,8,4,12]{1,4,3,2,0:T(8,128)} %get-tuple-element.57, f32[8,4,8,12]{3,1,0,2:T(4,128)S(1)} %get-tuple-element.56, pred[4,8,1152]{2,0,1:T(4,128)(4,1)S(1)} %compare_and_fusion, ...), kind=kOutput, calls=%fused_computation.23 | convolution fusion | flops 918552576 | bytes 24203264 | tf_op jit(solution)/shard_map/jtrhk,rkd->jtrhd/dot_general | solution.py:130
  109.3 0.9 copy.155
  110.4 0.2 bitcast_select_fusion.1
  110.6 24.9 %all_to_all.20 = bf16[16,4,8,1536]{3,2,1,0:T(8,128)(2,1)S(1)} all-to-all(bf16[16,4,8,1536]{3,2,1,0:T(8,128)(2,1)S(1)} %bitcast_select_fusion.1), channel_id=1, replica_groups=mesh['req'=8,'kv'=16] {'kv'}, dimensions={0} | all-to-all | bytes 3145728 | tf_op jit(solution)/shard_map/all_to_all | solution.py:160
  135.5 0.2 reduce_sum.322
  135.7 3.4 %multiply_reduce_fusion = (f32[32]{0:T(128)S(1)}, f32[32,1536]{1,0:T(8,128)S(1)}) fusion(bf16[1536,1536]{1,0:T(8,128)(2,1)} %param.23, bf16[4,8,1536]{2,1,0:T(8,128)(2,1)S(1)} %reduce_sum.322, f32[4,8,1536]{2,0,1:T(4,128)S(1)} %convert_bitcast_fusion), kind=kOutput, calls=%fused_computation.70 | convolution fusion | flops 151240672 | bytes 5210240 | tf_op jit(solution)/shard_map/dot_general | solution.py:165
  139.2 0.7 multiply_convert_fusion
  139.9 43.8 %all-gather.5.cloned.1.call-done = bf16[512,1536]{1,0:T(8,128)(2,1)} async-done(((bf16[32,1536]{1,0:T(8,128)(2,1)}), bf16[512,1536]{1,0:T(8,128)(2,1)}) %all-gather.5.cloned.1.call-update) | async-done | bytes 1572880 | tf_op jit(solution)/shard_map/all_gather | solution.py:169
  183.8 2.1 fusion.53
  185.8 4.2 %convolution_convert_fusion = bf16[512,1536]{1,0:T(8,128)(2,1)} fusion(bf16[288,1536]{1,0:T(8,128)(2,1)S(1)} %copy-done, bf16[512,1536]{1,0:T(8,128)(2,1)} %all-gather.5.cloned.1.call-done, bf16[1536,288]{0,1:T(8,128)(2,1)S(1)} %copy-done.3, f32[512,288]{0,1:T(8,128)S(1)} %fusion.53), kind=kOutput, calls=%fused_computation.12 | convolution fusion | flops 908230656 | bytes 5505024 | tf_op jit(solution)/shard_map/dot_general | solution.py:173
  190.1 4.7 %all-to-all-start.2 = ((bf16[16,32,1536]{2,1,0:T(8,128)(2,1)}), bf16[16,32,1536]{2,1,0:T(8,128)(2,1)S(1)}, u32[]{:S(2)}, u32[]{:S(2)}) async-start(bf16[16,32,1536]{2,1,0:T(8,128)(2,1)} %bitcast.168), calls=%async_computation.2 | async-start | bytes 3145728 | tf_op jit(solution)/shard_map/all_to_all | solution.py:175
  194.8 1.0 sort.32
  195.7 0.2 convert_reduce_fusion.3
  195.9 19.2 %all-to-all-done.2 = bf16[16,32,1536]{2,1,0:T(8,128)(2,1)S(1)} async-done(((bf16[16,32,1536]{2,1,0:T(8,128)(2,1)}), bf16[16,32,1536]{2,1,0:T(8,128)(2,1)S(1)}, u32[]{:S(2)}, u32[]{:S(2)}) %all-to-all-start.2) | async-done | bytes 1572896 | tf_op jit(solution)/shard_map/all_to_all | solution.py:175
  215.1 0.2 convert_reduce_fusion.1
  215.4 1.3 gather_fusion.4
  216.7 8.6 %all-to-all-start.3 = ((bf16[4,8,1,1536]{3,0,2,1:T(4,128)(2,1)}), bf16[4,8,1,1536]{3,0,2,1:T(4,128)(2,1)S(1)}, u32[]{:S(2)}, u32[]{:S(2)}) async-start(bf16[4,8,1,1536]{3,0,2,1:T(4,128)(2,1)} %bitcast.60), calls=%async_computation.3 | async-start | bytes 196608 | tf_op jit(solution)/shard_map/all_to_all | solution.py:182
  225.3 5.0 %all-to-all-done.3 = bf16[4,8,1,1536]{3,0,2,1:T(4,128)(2,1)S(1)} async-done(((bf16[4,8,1,1536]{3,0,2,1:T(4,128)(2,1)}), bf16[4,8,1,1536]{3,0,2,1:T(4,128)(2,1)S(1)}, u32[]{:S(2)}, u32[]{:S(2)}) %all-to-all-start.3) | async-done | bytes 98336 | tf_op jit(solution)/shard_map/all_to_all | solution.py:182
  230.3 0.6 gather_fusion.5
  230.9 0.7 copy.158
  (80 shorter events, 2.5 us)
Async XLA Ops:
  6.5 179.3 %copy-start = (bf16[288,1536]{1,0:T(8,128)(2,1)S(1)}, bf16[288,1536]{1,0:T(8,128)(2,1)}, u32[]{:S(2)}) copy-start(bf16[288,1536]{1,0:T(8,128)(2,1)} %param.27) | copy-start | bytes 2654212
  10.9 10.8 %all-to-all-start = ((bf16[4,8,1,1536]{3,0,2,1:T(4,128)(2,1)}), bf16[4,8,1,1536]{3,0,2,1:T(4,128)(2,1)S(1)}, u32[]{:S(2)}, u32[]{:S(2)}) async-start(bf16[4,8,1,1536]{3,0,2,1:T(4,128)(2,1)} %copy.127), calls=%async_computation | async-start | bytes 196608 | tf_op jit(solution)/shard_map/all_to_all | solution.py:80
  16.7 55.6 %all-gather.3.cloned.1.call-start = ((), (), s32[]{:S(2)}) async-start(), calls=%async_computation.4 | async-start | bytes 1949696 | tf_op jit(solution)/shard_map/all_gather | solution.py:88
  28.1 155.6 %all-gather.5.cloned.1.call-start = ((), (), s32[]{:S(2)}) async-start(), calls=%async_computation.5 | async-start | bytes 1671168 | tf_op jit(solution)/shard_map/all_gather | solution.py:169
  72.3 7.5 %slice-start = ((s8[4718592]{0:T(1024)(128)(4,1)}), s8[4194304]{0:T(1024)(128)(4,1)S(1)}, s32[]{:S(2)}) async-start(s8[4718592]{0:T(1024)(128)(4,1)} %bitcast.162), calls=%async_computation.6 | async-start | bytes 8388608
  76.2 3.6 %slice-start.1 = ((s8[4718592]{0:T(1024)(128)(4,1)}), s8[524288]{0:T(1024)(128)(4,1)S(1)}, s32[]{:S(2)}) async-start(s8[4718592]{0:T(1024)(128)(4,1)} %bitcast.162), calls=%async_computation.7 | async-start | bytes 1048576
  110.6 28.6 %copy-start.1 = (f32[1536]{0:T(1024)S(1)}, f32[1536]{0:T(1024)}, u32[]{:S(2)}) copy-start(f32[1536]{0:T(1024)} %param.24) | copy-start | bytes 18436
  135.7 48.1 %copy-start.2 = (bf16[1536,288]{0,1:T(8,128)(2,1)S(1)}, bf16[1536,288]{0,1:T(8,128)(2,1)}, u32[]{:S(2)}) copy-start(bf16[1536,288]{0,1:T(8,128)(2,1)} %param.25) | copy-start | bytes 2654212
  139.2 46.7 %copy-start.3 = (bf16[1536,288]{0,1:T(8,128)(2,1)S(1)}, bf16[1536,288]{0,1:T(8,128)(2,1)}, u32[]{:S(2)}) copy-start(bf16[1536,288]{0,1:T(8,128)(2,1)} %param.26) | copy-start | bytes 2654212
  190.1 25.0 %all-to-all-start.2 = ((bf16[16,32,1536]{2,1,0:T(8,128)(2,1)}), bf16[16,32,1536]{2,1,0:T(8,128)(2,1)S(1)}, u32[]{:S(2)}, u32[]{:S(2)}) async-start(bf16[16,32,1536]{2,1,0:T(8,128)(2,1)} %bitcast.168), calls=%async_computation.2 | async-start | bytes 3145728 | tf_op jit(solution)/shard_map/all_to_all | solution.py:175
  216.7 13.6 %all-to-all-start.3 = ((bf16[4,8,1,1536]{3,0,2,1:T(4,128)(2,1)}), bf16[4,8,1,1536]{3,0,2,1:T(4,128)(2,1)S(1)}, u32[]{:S(2)}, u32[]{:S(2)}) async-start(bf16[4,8,1,1536]{3,0,2,1:T(4,128)(2,1)} %bitcast.60), calls=%async_computation.3 | async-start | bytes 196608 | tf_op jit(solution)/shard_map/all_to_all | solution.py:182
Sparse Core Ops, SparseCore 0:
  28.3 44.0 all-gather.2
  140.1 43.6 all-gather.4
where the time goes:
time: 239 us; the launch traced here: 238 us
  waiting for transfers between devices  105 us (44%)
  matrix products  35.3 us (15%)
  blocking collectives  24.9 us (10%)
  local copies, waits for them, and re-layouts  20 us (8%)
  other arithmetic  20 us (8%)
  starting transfers between devices  19.1 us (8%)
  between operations  14 us (6%)
    all_gather x1, waiting for transfers between devices, on_device(): lax.all_gather(rms_round(residual, norm_mlp), 'kv', axis=0, tiled=True)  43.8 us
    all_gather x1, waiting for transfers between devices, on_device(): gathered = lax.all_gather(packed, 'kv', axis=0)  35.6 us
    all_to_all x1, blocking collectives, on_device(): lax.all_to_all(outgoing_att, 'kv', split_axis=0, concat_axis=0, tiled=True)  24.9 us
    all_to_all x1, waiting for transfers between devices, on_device(): lax.all_to_all(terms, 'kv', split_axis=0, concat_axis=0, tiled=True)  19.2 us
    reduce_sum x1, other arithmetic, on_device(): total_c = jnp.sum(weights.astype(jnp.float32), axis=-1)  11 us
    dot_general x1, matrix products, on_device(): jnp.einsum('jtrhk,rkd->jtrhd', weights, values, preferred_element_type=jn...  9.68 us
    all_to_all x1, starting transfers between devices, on_device(): lax.all_to_all(leaving, 'req', split_axis=1, concat_axis=1, tiled=True)  8.59 us
    dot_general x1, matrix products, on_device(): jnp.einsum('jtrhd,rkd->jtrhk', queries, keys, preferred_element_type=jnp....  8.53 us
  transfers between devices with their start and end apart: 5, of which 5 were waited for; matrix products, arithmetic and copies ran while one was open for 5% of the time, Pallas kernels for 0%

commit v1 on v0

--- a/solution.py
+++ b/solution.py
@@ -166,7 +166,12 @@
             attended_own.reshape(steps * rows, qwidth), w_out, preferred_element_type=jnp.float32
         )
     ).astype(jnp.bfloat16)
-    mlp_in = lax.all_gather(rms_round(residual, norm_mlp), "kv", axis=0, tiled=True)
+    mlp_in = jnp.concatenate(
+        lax.all_to_all(
+            jnp.stack([rms_round(residual, norm_mlp)] * lax.axis_size("kv")), "kv", 0, 0
+        ),
+        axis=0,
+    )
     gate = jnp.dot(mlp_in, w_gate, preferred_element_type=jnp.float32)
     upward = jnp.dot(mlp_in, w_up, preferred_element_type=jnp.float32)
     hidden = (jax.nn.gelu(gate, approximate=True) * upward).astype(jnp.bfloat16)

time: 239 us -> 213 us (0.89)
  waiting for transfers between devices: 105 us -> 59.4 us
  blocking collectives: 24.9 us -> 46.8 us
    all_gather x1 -> x0, waiting for transfers between devices: 43.8 us -> none  [on_device(): lax.all_gather(rms_round(residual, norm_mlp), 'kv', axis=0, tiled=True)]
    all_to_all x0 -> x1, blocking collectives: none -> 21.9 us  [on_device(): lax.all_to_all(jnp.stack([rms_round(residual, norm_mlp)] * lax.axis_size(...]
  transfers between devices with their start and end apart: 5 -> 4, of which waited for: 5 -> 4; matrix products, arithmetic and copies ran while one was open for 5% -> 6% of each run, Pallas kernels for 0% -> 0%
where the time goes in v1:
time: 213 us
  waiting for transfers between devices  59.4 us (28%)
  blocking collectives  46.8 us (22%)
  matrix products  33.6 us (16%)
  local copies, waits for them, and re-layouts  20.2 us (9%)
  other arithmetic  19.4 us (9%)
  starting transfers between devices  19.3 us (9%)
  between operations  13.9 us (7%)
    all_gather x1, waiting for transfers between devices, on_device(): gathered = lax.all_gather(packed, 'kv', axis=0)  35.7 us
    all_to_all x1, blocking collectives, on_device(): lax.all_to_all(outgoing_att, 'kv', split_axis=0, concat_axis=0, tiled=True)  24.9 us
    all_to_all x1, blocking collectives, on_device(): lax.all_to_all(jnp.stack([rms_round(residual, norm_mlp)] * lax.axis_size(...  21.9 us
    all_to_all x1, waiting for transfers between devices, on_device(): lax.all_to_all(terms, 'kv', split_axis=0, concat_axis=0, tiled=True)  17.1 us
    reduce_sum x1, other arithmetic, on_device(): total_c = jnp.sum(weights.astype(jnp.float32), axis=-1)  11 us
    all_to_all x1, starting transfers between devices, on_device(): lax.all_to_all(leaving, 'req', split_axis=1, concat_axis=1, tiled=True)  9.79 us
    dot_general x1, matrix products, on_device(): jnp.einsum('jtrhk,rkd->jtrhd', weights, values, preferred_element_type=jn...  9.68 us
    dot_general x1, matrix products, on_device(): jnp.einsum('jtrhd,rkd->jtrhk', queries, keys, preferred_element_type=jnp....  8.53 us
  transfers between devices with their start and end apart: 4, of which 4 were waited for; matrix products, arithmetic and copies ran while one was open for 6% of the time, Pallas kernels for 0%

profile of v1, /device:TPU:1, one launch (start us, length us, event | category | flops | bytes accessed | tf_op | source)
XLA Modules:
  0.0 212.6 jit_solution(10077016287649858722)
XLA Ops:
  6.5 0.8 reshape.457
  7.5 1.0 sort.31
  8.5 1.7 gather_fusion
  10.3 0.7 copy.127
  10.9 5.8 %all-to-all-start = ((bf16[4,8,1,1536]{3,0,2,1:T(4,128)(2,1)}), bf16[4,8,1,1536]{3,0,2,1:T(4,128)(2,1)S(1)}, u32[]{:S(2)}, u32[]{:S(2)}) async-start(bf16[4,8,1,1536]{3,0,2,1:T(4,128)(2,1)} %copy.127), calls=%async_computation | async-start | bytes 196608 | tf_op jit(solution)/shard_map/all_to_all | solution.py:80
  16.9 0.7 compare_select_fusion
  17.7 0.2 convert_reduce_fusion.4
  17.9 0.7 constant_dynamic-slice_fusion.4
  18.8 1.3 gather_fusion.3
  20.2 1.6 all-to-all-done
  21.7 0.6 gather_fusion.1
  22.4 0.1 multiply_reduce_fusion.1
  22.7 1.4 convolution_convert_fusion.2
  24.1 3.3 %convolution_convert_fusion.1 = bf16[32,1536]{1,0:T(8,128)(2,1)S(1)} fusion(bf16[1536,1536]{1,0:T(8,128)(2,1)} %param.21, f32[4,8,1536]{2,0,1:T(4,128)S(1)} %convert_bitcast_fusion, f32[1536]{0:T(1024)} %param.20, f32[32]{0:T(128)S(1)} %rsqrt.20), kind=kOutput, calls=%fused_computation.19 | convolution fusion | flops 151191552 | bytes 5019776 | tf_op jit(solution)/shard_map/dot_general | solution.py:85
  27.5 0.7 maximum_bitcast_fusion.4
  28.1 7.8 %gather_fusion.2 = bf16[72,128,256]{2,1,0:T(8,128)(2,1)} fusion(bf16[72,128,256]{2,1,0:T(8,128)(2,1)} %param.19, s32[1024]{0:T(1024)S(1)} %pad_clamp_fusion.3), kind=kCustom, calls=%fused_computation.2 | custom fusion | bytes 9437472 | tf_op jit(solution)/shard_map/gather | solution.py:115
  36.7 35.7 %all-gather.2.cloned.1.call-done = bf16[16,4,8,1792]{3,2,1,0:T(8,128)(2,1)} async-done(((bf16[1,4,8,1792]{3,2,1,0:T(8,128)(2,1)}), bf16[16,4,8,1792]{3,2,1,0:T(8,128)(2,1)}) %all-gather.2.cloned.1.call-update) | async-done | bytes 1835024 | tf_op jit(solution)/shard_map/all_gather | solution.py:88
  72.3 1.4 constant_dynamic-slice_fusion.1
  73.8 0.8 select_reduce_fusion.9
  75.2 0.3 maximum_bitcast_fusion.3
  75.6 0.6 maximum_bitcast_fusion
  76.2 0.4 pad_maximum_fusion
  76.6 0.7 fusion.52
  77.3 0.6 convert_reduce_fusion.2
  77.9 1.9 fusion.25
  79.8 8.5 %fusion = (f32[8,4,8,12]{3,1,0,2:T(4,128)S(1)}, f32[8,1152,8,4,12]{1,4,3,2,0:T(8,128)}) fusion(pred[4,8,1152]{2,0,1:T(4,128)(4,1)S(1)} %compare_and_fusion, bf16[8,4,8,12,128]{4,2,3,1,0:T(8,128)(2,1)S(1)} %slice_bitcast_fusion.6, bf16[8,1152,256]{2,1,0:T(8,128)(2,1)S(1)} %bitcast.165), kind=kOutput, calls=%fused_computation.10 | convolution fusion | flops 916583424 | bytes 17350656 | tf_op jit(solution)/shard_map/jtrhd,rkd->jtrhk/dot_general | solution.py:120
  88.3 11.0 %convert_reduce_fusion = f32[8,4,8,12]{3,1,0,2:T(4,128)S(1)} fusion(f32[8,4,8,12]{3,1,0,2:T(4,128)S(1)} %get-tuple-element.56, f32[8,1152,8,4,12]{1,4,3,2,0:T(8,128)} %get-tuple-element.57, pred[4,8,1152]{2,0,1:T(4,128)(4,1)S(1)} %compare_and_fusion), kind=kLoop, calls=%fused_computation.8 | loop fusion | flops 17691648 | bytes 14217216 | tf_op jit(solution)/shard_map/reduce_sum | solution.py:129
  99.3 0.2 fusion.32
  99.7 9.7 %fusion.6 = bf16[8,4,8,12,128]{4,3,1,0,2:T(8,128)(2,1)S(1)} fusion(f32[8,4,8,12,128]{4,3,1,0,2:T(8,128)} %fusion.25, bf16[8,1152,256]{2,1,0:T(8,128)(2,1)} %bitcast.162, f32[8,1152,8,4,12]{1,4,3,2,0:T(8,128)} %get-tuple-element.57, f32[8,4,8,12]{3,1,0,2:T(4,128)S(1)} %get-tuple-element.56, pred[4,8,1152]{2,0,1:T(4,128)(4,1)S(1)} %compare_and_fusion, ...), kind=kOutput, calls=%fused_computation.23 | convolution fusion | flops 918552576 | bytes 24203264 | tf_op jit(solution)/shard_map/jtrhk,rkd->jtrhd/dot_general | solution.py:130
  109.3 0.9 copy.155
  110.4 0.2 bitcast_select_fusion.1
  110.6 24.9 %all_to_all.25 = bf16[16,4,8,1536]{3,2,1,0:T(8,128)(2,1)S(1)} all-to-all(bf16[16,4,8,1536]{3,2,1,0:T(8,128)(2,1)S(1)} %bitcast_select_fusion.1), channel_id=1, replica_groups=mesh['req'=8,'kv'=16] {'kv'}, dimensions={0} | all-to-all | bytes 3145728 | tf_op jit(solution)/shard_map/all_to_all | solution.py:160
  135.5 0.2 reduce_sum.322
  135.8 3.4 %multiply_reduce_fusion = (f32[32]{0:T(128)S(1)}, f32[32,1536]{1,0:T(8,128)S(1)}) fusion(bf16[1536,1536]{1,0:T(8,128)(2,1)} %param.23, bf16[4,8,1536]{2,1,0:T(8,128)(2,1)S(1)} %reduce_sum.322, f32[4,8,1536]{2,0,1:T(4,128)S(1)} %convert_bitcast_fusion), kind=kOutput, calls=%fused_computation.70 | convolution fusion | flops 151240672 | bytes 5210240 | tf_op jit(solution)/shard_map/dot_general | solution.py:165
  139.3 0.1 stack.115
  139.5 21.9 %all_to_all.26 = bf16[16,32,1536]{2,1,0:T(8,128)(2,1)S(1)} all-to-all(bf16[16,32,1536]{2,1,0:T(8,128)(2,1)S(1)} %stack.115), channel_id=1, replica_groups=mesh['req'=8,'kv'=16] {'kv'}, dimensions={0} | all-to-all | bytes 3145728 | tf_op jit(solution)/shard_map/all_to_all | solution.py:170
  161.4 0.6 fusion.53
  162.1 4.0 %convolution_convert_fusion = bf16[512,1536]{1,0:T(8,128)(2,1)} fusion(bf16[288,1536]{1,0:T(8,128)(2,1)S(1)} %copy-done, bf16[512,1536]{1,0:T(8,128)(2,1)S(1)} %bitcast.171, bf16[1536,288]{0,1:T(8,128)(2,1)} %param.26, f32[512,288]{0,1:T(8,128)S(1)} %fusion.53), kind=kOutput, calls=%fused_computation.12 | convolution fusion | flops 908230656 | bytes 5505024 | tf_op jit(solution)/shard_map/dot_general | solution.py:178
  166.1 3.7 %all-to-all-start.3 = ((bf16[16,32,1536]{2,1,0:T(8,128)(2,1)}), bf16[16,32,1536]{2,1,0:T(8,128)(2,1)S(1)}, u32[]{:S(2)}, u32[]{:S(2)}) async-start(bf16[16,32,1536]{2,1,0:T(8,128)(2,1)} %bitcast.169), calls=%async_computation.3 | async-start | bytes 3145728 | tf_op jit(solution)/shard_map/all_to_all | solution.py:180
  169.8 1.0 sort.32
  170.8 0.2 convert_reduce_fusion.3
  171.0 17.1 %all-to-all-done.3 = bf16[16,32,1536]{2,1,0:T(8,128)(2,1)S(1)} async-done(((bf16[16,32,1536]{2,1,0:T(8,128)(2,1)}), bf16[16,32,1536]{2,1,0:T(8,128)(2,1)S(1)}, u32[]{:S(2)}, u32[]{:S(2)}) %all-to-all-start.3) | async-done | bytes 1572896 | tf_op jit(solution)/shard_map/all_to_all | solution.py:180
  188.1 0.2 convert_reduce_fusion.1
  188.4 1.3 gather_fusion.4
  189.7 9.8 %all-to-all-start.4 = ((bf16[4,8,1,1536]{3,0,2,1:T(4,128)(2,1)}), bf16[4,8,1,1536]{3,0,2,1:T(4,128)(2,1)S(1)}, u32[]{:S(2)}, u32[]{:S(2)}) async-start(bf16[4,8,1,1536]{3,0,2,1:T(4,128)(2,1)} %bitcast.61), calls=%async_computation.4 | async-start | bytes 196608 | tf_op jit(solution)/shard_map/all_to_all | solution.py:187
  199.5 5.0 %all-to-all-done.4 = bf16[4,8,1,1536]{3,0,2,1:T(4,128)(2,1)S(1)} async-done(((bf16[4,8,1,1536]{3,0,2,1:T(4,128)(2,1)}), bf16[4,8,1,1536]{3,0,2,1:T(4,128)(2,1)S(1)}, u32[]{:S(2)}, u32[]{:S(2)}) %all-to-all-start.4) | async-done | bytes 98336 | tf_op jit(solution)/shard_map/all_to_all | solution.py:187
  204.4 0.6 gather_fusion.5
  205.1 0.7 copy.158
  (77 shorter events, 2.5 us)
Async XLA Ops:
  6.5 155.5 %copy-start = (bf16[288,1536]{1,0:T(8,128)(2,1)S(1)}, bf16[288,1536]{1,0:T(8,128)(2,1)}, u32[]{:S(2)}) copy-start(bf16[288,1536]{1,0:T(8,128)(2,1)} %param.27) | copy-start | bytes 2654212
  10.9 10.8 %all-to-all-start = ((bf16[4,8,1,1536]{3,0,2,1:T(4,128)(2,1)}), bf16[4,8,1,1536]{3,0,2,1:T(4,128)(2,1)S(1)}, u32[]{:S(2)}, u32[]{:S(2)}) async-start(bf16[4,8,1,1536]{3,0,2,1:T(4,128)(2,1)} %copy.127), calls=%async_computation | async-start | bytes 196608 | tf_op jit(solution)/shard_map/all_to_all | solution.py:80
  16.7 55.6 %all-gather.2.cloned.1.call-start = ((), (), s32[]{:S(2)}) async-start(), calls=%async_computation.5 | async-start | bytes 1949696 | tf_op jit(solution)/shard_map/all_gather | solution.py:88
  72.3 7.5 %slice-start = ((s8[4718592]{0:T(1024)(128)(4,1)}), s8[4194304]{0:T(1024)(128)(4,1)S(1)}, s32[]{:S(2)}) async-start(s8[4718592]{0:T(1024)(128)(4,1)} %bitcast.163), calls=%async_computation.6 | async-start | bytes 8388608
  76.2 3.6 %slice-start.1 = ((s8[4718592]{0:T(1024)(128)(4,1)}), s8[524288]{0:T(1024)(128)(4,1)S(1)}, s32[]{:S(2)}) async-start(s8[4718592]{0:T(1024)(128)(4,1)} %bitcast.163), calls=%async_computation.7 | async-start | bytes 1048576
  110.6 28.6 %copy-start.1 = (f32[1536]{0:T(1024)S(1)}, f32[1536]{0:T(1024)}, u32[]{:S(2)}) copy-start(f32[1536]{0:T(1024)} %param.24) | copy-start | bytes 18436
  135.7 25.7 %copy-start.2 = (bf16[1536,288]{0,1:T(8,128)(2,1)S(1)}, bf16[1536,288]{0,1:T(8,128)(2,1)}, u32[]{:S(2)}) copy-start(bf16[1536,288]{0,1:T(8,128)(2,1)} %param.25) | copy-start | bytes 2654212
  166.1 22.0 %all-to-all-start.3 = ((bf16[16,32,1536]{2,1,0:T(8,128)(2,1)}), bf16[16,32,1536]{2,1,0:T(8,128)(2,1)S(1)}, u32[]{:S(2)}, u32[]{:S(2)}) async-start(bf16[16,32,1536]{2,1,0:T(8,128)(2,1)} %bitcast.169), calls=%async_computation.3 | async-start | bytes 3145728 | tf_op jit(solution)/shard_map/all_to_all | solution.py:180
  189.7 14.8 %all-to-all-start.4 = ((bf16[4,8,1,1536]{3,0,2,1:T(4,128)(2,1)}), bf16[4,8,1,1536]{3,0,2,1:T(4,128)(2,1)S(1)}, u32[]{:S(2)}, u32[]{:S(2)}) async-start(bf16[4,8,1,1536]{3,0,2,1:T(4,128)(2,1)} %bitcast.61), calls=%async_computation.4 | async-start | bytes 196608 | tf_op jit(solution)/shard_map/all_to_all | solution.py:187
Sparse Core Ops, SparseCore 0:
  28.3 44.0 all-gather.1
